TPU v7x, 32 devices: a whole 2x2x4 slice. The times are simulated.
32 devices in a mesh: groups: 2 (over y), rows: 4 (over z), cols: 4 (over x, core).
Axes of the slice: x: 2, y: 2, z: 4, core: 2. Of those that a mesh axis runs over, the one named last changes fastest.
Arguments:
- points: bfloat16 [6144, 128], P(('groups', 'rows', 'cols')), parts along dimension 0, as said below
- solution: float32 [6144, 128], P(('groups', 'rows', 'cols')), parts along dimension 0, may hold values from -6 to 6
- targets: float32 [6144, 128], P(('groups', 'rows', 'cols')), parts along dimension 0, may hold values from -40 to 40, as said below
- inducing: int32 [2048], P('groups'), parts along dimension 0, may hold values from 0 to 3071, as said below
- woodbury_inverse: float32 [2048, 1024], P('groups'), parts along dimension 0, may hold values from -1 to 7, as said below
Outputs:
- new_solution: float32 [6144, 128], P(('groups', 'rows', 'cols')), parts along dimension 0
- residual: float32 [6144, 128], P(('groups', 'rows', 'cols')), parts along dimension 0
- relative_norm: float32 [256], P('groups'), parts along dimension 0
There are 2 independent parts, one for each index of `groups`. A program takes and returns all parts, laid end to end along the dimension named above; each array names one. Nothing has to cross between parts.
Inputs may be any that keep to these rules, and one draw needn't show every extreme that they name: `points`: input locations. targets of each right-hand side have their own scale. `inducing`: indices into this problem's points. `woodbury_inverse`: symmetric.
All inputs are finite; a program needn't handle non-finite values.
Results may differ from a plain program's by a relative error of at most 0.0031.
Values may be sent and summed in bfloat16 or wider, within the bound.
No kernel may reach another device: no remote copies, remote signals or barrier semaphores. Data moves between devices by JAX's collectives and lax.ppermute only.
A program may use at most 64 MiB of HBM per device.

v0:
```python
import jax
import jax.numpy as jnp
from jax import lax
from jax.sharding import PartitionSpec as P

F = 128
noise_level = 0.5
COLUMN_CHUNK = 3072


def square_norms(values):
    return jnp.sum(jnp.square(values.astype(jnp.float32)), axis=1)


def rbf_tile(left_x, left_sq, right_x, right_sq, gamma):
    inner = lax.dot_general(
        left_x, right_x, (((1,), (1,)), ((), ())), preferred_element_type=jnp.float32
    )
    return jnp.exp(-gamma * (left_sq[:, None] + right_sq[None, :] - 2.0 * inner)).astype(
        jnp.bfloat16
    )


def kernel_product(own_x, own_sq, all_x, all_sq, all_v, gamma):
    total = all_x.shape[0]
    chunk = min(COLUMN_CHUNK, total)
    if total % chunk != 0:
        chunk = total
    steps = total // chunk

    def piece(start):
        x = lax.dynamic_slice_in_dim(all_x, start, chunk, 0)
        s = lax.dynamic_slice_in_dim(all_sq, start, chunk, 0)
        v = lax.dynamic_slice_in_dim(all_v, start, chunk, 0)
        k = rbf_tile(own_x, own_sq, x, s, gamma)
        return jnp.dot(k, v, preferred_element_type=jnp.float32)

    if steps == 1:
        return piece(0)

    def body(i, acc):
        return acc + piece(i * chunk)

    init = jnp.zeros((own_x.shape[0], all_v.shape[1]), jnp.float32)
    return lax.fori_loop(0, steps, body, init)


def local(points, solution, targets, inducing, woodbury_inverse):
    gamma = 2.5 / F
    solution_b = solution.astype(jnp.bfloat16)
    packed = jnp.concatenate([points, solution_b], axis=1)
    gathered = lax.all_gather(packed, ("rows", "cols"), axis=0, tiled=True)
    all_x = gathered[:, :F]
    all_v = gathered[:, F:]
    all_sq = square_norms(all_x)
    own_sq = square_norms(points)
    kp = kernel_product(points, own_sq, all_x, all_sq, all_v, gamma)
    residual = targets - kp - noise_level * solution
    centers = jnp.take(all_x, inducing, axis=0)
    cross = rbf_tile(points, own_sq, centers, square_norms(centers), gamma)
    residual_b = residual.astype(jnp.bfloat16)
    projected_local = lax.dot_general(
        cross, residual_b, (((0,), (0,)), ((), ())), preferred_element_type=jnp.float32
    )
    res_local = jnp.sum(residual * residual, axis=0)
    tar_local = jnp.sum(targets * targets, axis=0)
    stacked = jnp.concatenate([projected_local, res_local[None], tar_local[None]], axis=0)
    summed = lax.psum(stacked, ("rows", "cols"))
    m = projected_local.shape[0]
    projected = summed[:m]
    res_sq = summed[m]
    tar_sq = summed[m + 1]
    weights = jnp.dot(woodbury_inverse, projected, precision=lax.Precision.HIGHEST)
    correction = jnp.dot(cross, weights.astype(jnp.bfloat16), preferred_element_type=jnp.float32)
    new_solution = solution + (residual - correction) / noise_level
    relative_norm = jnp.sqrt(res_sq / (tar_sq + 1e-06))
    return (new_solution, residual, relative_norm)


def solution(mesh):
    return jax.shard_map(
        local,
        mesh=mesh,
        in_specs=(
            P(("groups", "rows", "cols"), None),
            P(("groups", "rows", "cols"), None),
            P(("groups", "rows", "cols"), None),
            P("groups"),
            P("groups", None),
        ),
        out_specs=(
            P(("groups", "rows", "cols"), None),
            P(("groups", "rows", "cols"), None),
            P("groups"),
        ),
        check_vma=False,
    )
```

profile of v0, /device:TPU:0, one launch (start us, length us, event | category | flops | bytes accessed | tf_op | source)
XLA Modules:
  0.0 167.1 jit_solution(9886940378741417680)
XLA Ops:
  7.2 0.0 all-gather.2.cloned.1.call-start
  7.2 0.9 convert_element_type.26
  8.1 0.0 copy-start.3
  8.1 1.5 pad_maximum_fusion
  9.6 0.0 all-gather.2.cloned.1.call-update
  9.7 0.0 all-reduce.2.cloned.1.call-start
  9.7 0.9 multiply_reduce_fusion.4
  10.6 0.9 multiply_reduce_fusion.2
  11.6 0.7 compare_and_fusion
  12.3 0.7 fusion.23
  12.9 40.2 %all-gather.2.cloned.1.call-done = bf16[3072,256]{1,0:T(8,128)(2,1)} async-done(((bf16[192,256]{1,0:T(8,128)(2,1)}), bf16[3072,256]{1,0:T(8,128)(2,1)}) %all-gather.2.cloned.1.call-update) | async-done | bytes 1572880 | tf_op jit(solution)/shard_map/all_gather | solution.py:52
  53.2 0.0 slice-start
  53.2 1.1 slice-done
  54.3 0.0 copy-start
  54.3 0.0 copy-start.1
  54.3 0.0 copy-start.4
  54.3 3.2 %gather_fusion = bf16[1024,128]{1,0:T(8,128)(2,1)S(1)} fusion(bf16[3072,128]{1,0:T(8,128)(2,1)S(1)} %slice-done, s32[1024]{0:T(1024)S(1)} %fusion.23), kind=kCustom, calls=%fused_computation | custom fusion | bytes 528384 | tf_op jit(solution)/shard_map/jit(_take)/gather | solution.py:59
  57.5 0.4 multiply_reduce_fusion.1
  57.9 0.0 copy-done.3
  57.9 0.5 fusion.10
  58.4 0.0 copy-done
  58.4 0.5 multiply_reduce_fusion
  58.9 0.0 copy-done.1
  58.9 0.0 copy-done.4
  58.9 1.0 multiply_reduce_fusion.3
  59.9 0.0 copy-start.2
  59.9 0.3 fusion.21
  60.2 1.5 concatenate.7
  61.7 0.0 all-reduce.2.cloned.1.call-update
  61.7 89.5 %all-reduce.2.cloned.1.call-done = f32[1026,128]{1,0:T(8,128)} async-done(((f32[1026,128]{1,0:T(8,128)}), f32[1026,128]{1,0:T(8,128)}) %all-reduce.2.cloned.1.call-update) | async-done | bytes 525328 | tf_op jit(solution)/shard_map/psum | solution.py:68
  151.2 6.8 %convolution_convert_fusion = bf16[128,1024]{1,0:T(8,128)(2,1)S(1)} fusion(f32[1024,1024]{1,0:T(8,128)} %param.9, f32[1026,128]{1,0:T(8,128)} %all-reduce.2.cloned.1.call-done), kind=kOutput, calls=%fused_computation.15 | convolution fusion | flops 1610743808 | bytes 4980736 | tf_op jit(solution)/shard_map/dot_general | solution.py:73
  158.1 0.0 copy-done.2
  158.1 0.9 fusion.18
  159.0 1.3 sqrt_bitcast_fusion
Async XLA Ops:
  7.2 46.0 %all-gather.2.cloned.1.call-start = ((), (), s32[]{:S(2)}) async-start(), calls=%async_computation | async-start | bytes 1671168 | tf_op jit(solution)/shard_map/all_gather | solution.py:52
  8.1 49.8 %copy-start.3 = (bf16[192,128]{1,0:T(8,128)(2,1)S(1)}, bf16[192,128]{1,0:T(8,128)(2,1)}, u32[]{:S(2)}) copy-start(bf16[192,128]{1,0:T(8,128)(2,1)} %param.5) | copy-start | bytes 147460
  9.7 141.6 %all-reduce.2.cloned.1.call-start = ((), (), s32[]{:S(2)}) async-start(), calls=%async_computation.1 | async-start | bytes 1056768 | tf_op jit(solution)/shard_map/psum | solution.py:68
  53.2 1.1 slice-start
  54.3 4.1 %copy-start = (bf16[3072,256]{1,0:T(8,128)(2,1)S(1)}, bf16[3072,256]{1,0:T(8,128)(2,1)}, u32[]{:S(2)}) copy-start(bf16[3072,256]{1,0:T(8,128)(2,1)} %all-gather.2.cloned.1.call-done) | copy-start | bytes 4718596
  54.3 4.5 %copy-start.1 = (f32[192,128]{1,0:T(8,128)S(1)}, f32[192,128]{1,0:T(8,128)}, u32[]{:S(2)}) copy-start(f32[192,128]{1,0:T(8,128)} %param.6) | copy-start | bytes 294916
  54.3 4.6 %copy-start.4 = (f32[192,128]{1,0:T(8,128)S(1)}, f32[192,128]{1,0:T(8,128)}, u32[]{:S(2)}) copy-start(f32[192,128]{1,0:T(8,128)} %param.7) | copy-start | bytes 294916
  59.9 98.2 %copy-start.2 = (f32[192,128]{1,0:T(8,128)}, f32[192,128]{1,0:T(8,128)S(1)}, u32[]{:S(2)}) copy-start(f32[192,128]{1,0:T(8,128)S(1)} %get-tuple-element.4) | copy-start | bytes 294916
Sparse Core Ops, SparseCore 0:
  10.8 42.3 all-gather.1
  61.9 89.3 all-reduce.1
where the time goes:
time: 168 us; the launch traced here: 167 us
  waiting for transfers between devices  130 us (77%)
  between operations  14.1 us (8%)
  matrix products  9.53 us (6%)
  other arithmetic  7.78 us (5%)
  local copies, waits for them, and re-layouts  5.84 us (3%)
    psum x1, waiting for transfers between devices, local(): summed = lax.psum(stacked, ('rows', 'cols'))  89.5 us
    all_gather x1, waiting for transfers between devices, local(): gathered = lax.all_gather(packed, ('rows', 'cols'), axis=0, tiled=True)  40.2 us
    dot_general x1, matrix products, local(): jnp.dot(woodbury_inverse, projected, precision=lax.Precision.HIGHEST)  6.82 us
  transfers between devices with their start and end apart: 2, of which 2 were waited for; matrix products, arithmetic and copies ran while one was open for 2% of the time, Pallas kernels for 0%

commit v1 on v0

--- a/solution.py
+++ b/solution.py
@@ -65,7 +65,8 @@
     res_local = jnp.sum(residual * residual, axis=0)
     tar_local = jnp.sum(targets * targets, axis=0)
     stacked = jnp.concatenate([projected_local, res_local[None], tar_local[None]], axis=0)
-    summed = lax.psum(stacked, ("rows", "cols"))
+    parts = lax.all_gather(stacked, ("rows", "cols"))
+    summed = jnp.sum(parts, axis=0)
     m = projected_local.shape[0]
     projected = summed[:m]
     res_sq = summed[m]

time: 168 us -> 155 us (0.923)
  waiting for transfers between devices: 130 us -> 114 us
  other arithmetic: 7.78 us -> 10.9 us
    psum x1 -> x0, waiting for transfers between devices: 89.5 us -> none  [local(): summed = lax.psum(stacked, ('rows', 'cols'))]
    all_gather x0 -> x1, waiting for transfers between devices: none -> 73.6 us  [local(): parts = lax.all_gather(stacked, ('rows', 'cols'))]
    reduce_sum x0 -> x1, other arithmetic: none -> 3.84 us  [local(): summed = jnp.sum(parts, axis=0)]
where the time goes in v1:
time: 155 us; the launch traced here: 154 us
  waiting for transfers between devices  114 us (74%)
  between operations  14.1 us (9%)
  other arithmetic  10.9 us (7%)
  matrix products  9.37 us (6%)
  local copies, waits for them, and re-layouts  5.87 us (4%)
    all_gather x1, waiting for transfers between devices, local(): parts = lax.all_gather(stacked, ('rows', 'cols'))  73.6 us
    all_gather x1, waiting for transfers between devices, local(): gathered = lax.all_gather(packed, ('rows', 'cols'), axis=0, tiled=True)  40.2 us
    dot_general x1, matrix products, local(): jnp.dot(woodbury_inverse, projected, precision=lax.Precision.HIGHEST)  6.67 us
    reduce_sum x1, other arithmetic, local(): summed = jnp.sum(parts, axis=0)  3.84 us
    gather x1, local copies, waits for them, and re-layouts, local(): centers = jnp.take(all_x, inducing, axis=0)  3.2 us
  transfers between devices with their start and end apart: 2, of which 2 were waited for; matrix products, arithmetic and copies ran while one was open for 2% of the time, Pallas kernels for 0%

profile of v1, /device:TPU:0, one launch (start us, length us, event | category | flops | bytes accessed | tf_op | source)
XLA Modules:
  0.0 154.1 jit_solution(15783901470251403249)
XLA Ops:
  7.2 0.0 all-gather.5.cloned.1.call-start
  7.2 0.9 convert_element_type.26
  8.1 0.0 copy-start.3
  8.1 1.5 pad_maximum_fusion
  9.6 0.0 all-gather.5.cloned.1.call-update
  9.7 0.0 all-gather.7.cloned.1.call-start
  9.7 0.9 multiply_reduce_fusion.4
  10.6 0.9 multiply_reduce_fusion.2
  11.6 0.7 compare_and_fusion
  12.3 0.7 fusion.23
  12.9 40.2 %all-gather.5.cloned.1.call-done = bf16[3072,256]{1,0:T(8,128)(2,1)} async-done(((bf16[192,256]{1,0:T(8,128)(2,1)}), bf16[3072,256]{1,0:T(8,128)(2,1)}) %all-gather.5.cloned.1.call-update) | async-done | bytes 1572880 | tf_op jit(solution)/shard_map/all_gather | solution.py:52
  53.2 0.0 slice-start
  53.2 1.1 slice-done
  54.3 0.0 copy-start
  54.3 0.0 copy-start.1
  54.3 0.0 copy-start.4
  54.3 3.2 %gather_fusion = bf16[1024,128]{1,0:T(8,128)(2,1)S(1)} fusion(bf16[3072,128]{1,0:T(8,128)(2,1)S(1)} %slice-done, s32[1024]{0:T(1024)S(1)} %fusion.23), kind=kCustom, calls=%fused_computation | custom fusion | bytes 528384 | tf_op jit(solution)/shard_map/jit(_take)/gather | solution.py:59
  57.5 0.4 multiply_reduce_fusion.1
  57.9 0.0 copy-done.3
  57.9 0.5 fusion.10
  58.4 0.0 copy-done
  58.4 0.5 multiply_reduce_fusion
  58.9 0.0 copy-done.1
  58.9 0.0 copy-done.4
  58.9 1.0 multiply_reduce_fusion.3
  59.9 0.0 copy-start.2
  59.9 0.3 fusion.21
  60.2 1.5 concatenate.7
  61.7 0.0 all-gather.7.cloned.1.call-update
  61.8 73.6 %all-gather.7.cloned.1.call-done = f32[16,1026,128]{2,1,0:T(8,128)} async-done(((f32[1,1026,128]{2,1,0:T(8,128)}), f32[16,1026,128]{2,1,0:T(8,128)}) %all-gather.7.cloned.1.call-update) | async-done | bytes 8405008 | tf_op jit(solution)/shard_map/all_gather | solution.py:68
  135.3 3.8 %reduce_sum.59 = f32[1026,128]{1,0:T(8,128)S(1)} reduce(f32[16,1026,128]{2,1,0:T(8,128)} %all-gather.7.cloned.1.call-done, f32[]{:T(128)} %constant.9.clone.1), dimensions={0}, to_apply=%region_5.6 | reduce | flops 1969920 | bytes 8930308 | tf_op jit(solution)/shard_map/reduce_sum | solution.py:69
  139.2 0.5 sqrt_bitcast_fusion
  139.7 6.7 %convolution_convert_fusion = bf16[128,1024]{1,0:T(8,128)(2,1)S(1)} fusion(f32[1024,1024]{1,0:T(8,128)} %param.9, f32[1026,128]{1,0:T(8,128)S(1)} %reduce_sum.59), kind=kOutput, calls=%fused_computation.15 | convolution fusion | flops 1610743808 | bytes 4980736 | tf_op jit(solution)/shard_map/dot_general | solution.py:74
  146.4 0.0 copy-done.2
  146.4 0.9 fusion.18
Async XLA Ops:
  7.2 46.0 %all-gather.5.cloned.1.call-start = ((), (), s32[]{:S(2)}) async-start(), calls=%async_computation | async-start | bytes 1671168 | tf_op jit(solution)/shard_map/all_gather | solution.py:52
  8.1 49.8 %copy-start.3 = (bf16[192,128]{1,0:T(8,128)(2,1)S(1)}, bf16[192,128]{1,0:T(8,128)(2,1)}, u32[]{:S(2)}) copy-start(bf16[192,128]{1,0:T(8,128)(2,1)} %param.5) | copy-start | bytes 147460
  9.7 125.7 %all-gather.7.cloned.1.call-start = ((), (), s32[]{:S(2)}) async-start(), calls=%async_computation.1 | async-start | bytes 8982528 | tf_op jit(solution)/shard_map/all_gather | solution.py:68
  53.2 1.1 slice-start
  54.3 4.1 %copy-start = (bf16[3072,256]{1,0:T(8,128)(2,1)S(1)}, bf16[3072,256]{1,0:T(8,128)(2,1)}, u32[]{:S(2)}) copy-start(bf16[3072,256]{1,0:T(8,128)(2,1)} %all-gather.5.cloned.1.call-done) | copy-start | bytes 4718596
  54.3 4.5 %copy-start.1 = (f32[192,128]{1,0:T(8,128)S(1)}, f32[192,128]{1,0:T(8,128)}, u32[]{:S(2)}) copy-start(f32[192,128]{1,0:T(8,128)} %param.6) | copy-start | bytes 294916
  54.3 4.6 %copy-start.4 = (f32[192,128]{1,0:T(8,128)S(1)}, f32[192,128]{1,0:T(8,128)}, u32[]{:S(2)}) copy-start(f32[192,128]{1,0:T(8,128)} %param.7) | copy-start | bytes 294916
  59.9 86.5 %copy-start.2 = (f32[192,128]{1,0:T(8,128)}, f32[192,128]{1,0:T(8,128)S(1)}, u32[]{:S(2)}) copy-start(f32[192,128]{1,0:T(8,128)S(1)} %get-tuple-element.4) | copy-start | bytes 294916
Sparse Core Ops, SparseCore 0:
  10.8 42.3 all-gather.4
  61.9 73.3 all-gather.6
